TPU v7x, 256 devices: a whole 4x4x8 slice. The times are simulated.
256 devices in a mesh: blk: 32 (over x, y, core), req: 8 (over z).
Axes of the slice: x: 4, y: 4, z: 8, core: 2. Of those that a mesh axis runs over, the one named last changes fastest.
Arguments:
- patches: bfloat16 [6144, 1408], P('req')
- vis_ln_gain: bfloat16 [1408], replicated, may hold values from 0.25 to 4
- vis_ln_bias: bfloat16 [1408], replicated, may hold values from -3 to 3
- vis_up: bfloat16 [1408, 6144], P(None, 'blk'), may hold values from -0.15625 to 0.15625
- vis_up_bias: bfloat16 [6144], P('blk'), may hold values from -3 to 3
- vis_down: bfloat16 [6144, 1408], P('blk'), may hold values from -0.15625 to 0.15625
- vis_down_bias: bfloat16 [1408], replicated, may hold values from -3 to 3
- merge_gain: bfloat16 [1408], replicated, may hold values from 0.099609375 to 1.8984375
- merge_proj: bfloat16 [5632, 4096], P(None, 'blk'), may hold values from -0.078125 to 0.078125
- merge_proj_bias: bfloat16 [4096], P('blk'), may hold values from -3 to 3
- image_dest: int32 [1536], replicated, may hold values from 0 to 8191, as said below
- text_embed: bfloat16 [8192, 4096], P('req', 'blk')
- segment_ids: int32 [8, 1024], P('req'), may hold values from 0 to 3, never falling along the last dimension, each value on 1 to 512 neighbouring positions
- text_gain: bfloat16 [4096], replicated, may hold values from 0.099609375 to 1.8984375
- query_weight: bfloat16 [4096, 4096], P(None, 'blk')
- key_weight: bfloat16 [4096, 4096], P(None, 'blk')
- value_weight: bfloat16 [4096, 4096], P(None, 'blk'), may hold values from -0.09375 to 0.09375
- out_weight: bfloat16 [4096, 4096], P('blk'), may hold values from -0.1875 to 0.1875
Outputs:
- hidden_out: bfloat16 [8192, 4096], P(('req', 'blk'))
Inputs may be any that keep to these rules, and one draw needn't show every extreme that they name: image_dest holds distinct positions; each group of 1024 positions receives exactly 192 image rows, and of one group's 192 image rows at most 66 go to one group of positions, exactly 66 for one group. `segment_ids`: each row has 4 requests as runs of equal, non-decreasing ids, each of 1 to 512 tokens, one exactly 512.
All inputs are finite; a program needn't handle non-finite values.
Results may differ from a plain program's by a relative error of at most 0.04.
Values may be sent and summed in bfloat16 or wider, within the bound.
No kernel may reach another device: no remote copies, remote signals or barrier semaphores. Data moves between devices by JAX's collectives and lax.ppermute only.
A program may use at most 128 MiB of HBM per device.

v0:
```python
import jax
import jax.numpy as jnp
from jax import lax
from jax.sharding import PartitionSpec as P

HEAD = 128


def layer_norm(values, gain_vector, shift_vector):
    centre = jnp.mean(values, axis=-1, keepdims=True)
    centred = values - centre
    spread = jnp.mean(centred * centred, axis=-1, keepdims=True)
    result = centred * lax.rsqrt(spread + 1e-06) * gain_vector.astype(jnp.float32)
    if shift_vector is None:
        return result
    return result + shift_vector.astype(jnp.float32)


def rotate(values, positions):
    half_size = HEAD // 2
    frequency = 10000.0 ** (-2.0 * jnp.arange(half_size, dtype=jnp.float32) / HEAD)
    angles = positions.astype(jnp.float32)[:, None] * frequency[None, :]
    cosine = jnp.cos(angles)[:, None, :]
    sine_table = jnp.sin(angles)[:, None, :]
    by_head = values.reshape(values.shape[0], -1, HEAD)
    first_half = by_head[..., :half_size]
    second_half = by_head[..., half_size:]
    turned = jnp.concatenate(
        [
            first_half * cosine - second_half * sine_table,
            second_half * cosine + first_half * sine_table,
        ],
        axis=-1,
    )
    return turned.reshape(values.shape)


def causal_setup(segments):
    length = segments.shape[0]
    column_ids = jnp.arange(length)
    same_request = segments[:, None] == segments[None, :]
    earlier = column_ids[None, :] < column_ids[:, None]
    positions = jnp.sum(same_request & earlier, axis=1)
    allowed = same_request & (column_ids[None, :] <= column_ids[:, None])
    return (positions, allowed)


def attend(queries, keys, values, allowed):
    row_count = queries.shape[0]
    key_count = keys.shape[0]
    query_heads = queries.reshape(row_count, -1, HEAD)
    key_heads = keys.reshape(key_count, -1, HEAD)
    value_heads = values.reshape(key_count, -1, HEAD)
    scores = jnp.einsum(
        "thd,shd->hts", query_heads, key_heads, preferred_element_type=jnp.float32
    ) * HEAD ** (-0.5)
    scores = jnp.where(allowed[None, :, :], scores, -jnp.inf)
    top_score = jnp.max(scores, axis=-1, keepdims=True)
    weights = jnp.exp(scores - top_score)
    weights = (weights / jnp.sum(weights, axis=-1, keepdims=True)).astype(jnp.bfloat16)
    mixed = jnp.einsum("hts,shd->thd", weights, value_heads, preferred_element_type=jnp.float32)
    return mixed.astype(jnp.bfloat16).reshape(row_count, -1)


def body(
    patches,
    vis_ln_gain,
    vis_ln_bias,
    vis_up,
    vis_up_bias,
    vis_down,
    vis_down_bias,
    merge_gain,
    merge_proj,
    merge_proj_bias,
    image_dest,
    text_embed,
    segment_ids,
    text_gain,
    query_weight,
    key_weight,
    value_weight,
    out_weight,
):
    blk_count = lax.axis_size("blk")
    req_count = lax.axis_size("req")
    blk_index = lax.axis_index("blk")
    req_index = lax.axis_index("req")
    vis_width = patches.shape[1]
    patch_rows = patches.astype(jnp.float32)
    normed = layer_norm(patch_rows, vis_ln_gain, vis_ln_bias).astype(jnp.bfloat16)
    pre_act = jnp.dot(normed, vis_up, preferred_element_type=jnp.float32) + vis_up_bias.astype(
        jnp.float32
    )
    hidden = jax.nn.gelu(pre_act, approximate=False).astype(jnp.bfloat16)
    summed = lax.psum(
        jnp.dot(hidden, vis_down, preferred_element_type=jnp.float32).astype(jnp.bfloat16), "blk"
    ).astype(jnp.float32)
    vis_out = patches.astype(jnp.float32) + summed + vis_down_bias.astype(jnp.float32)
    normed = layer_norm(vis_out, merge_gain, None).astype(jnp.bfloat16)
    image_cols = jnp.dot(
        normed.reshape(-1, 4 * vis_width), merge_proj, preferred_element_type=jnp.float32
    )
    image_cols = (image_cols + merge_proj_bias.astype(jnp.float32)).astype(jnp.bfloat16)
    image_count = image_cols.shape[0]
    col_width = image_cols.shape[1]
    tok_grp = text_embed.shape[0]
    dest_group = image_dest // tok_grp
    dest_local = image_dest - dest_group * tok_grp
    target = jnp.where(dest_group == req_index, dest_local, tok_grp)
    filler = jnp.zeros((1, col_width), jnp.bfloat16)
    capacity = image_count // 4 + 3 * image_count // 4 // req_count
    by_source = dest_group.reshape(req_count, image_count)
    one_hot = (
        by_source[:, :, None] == jnp.arange(req_count, dtype=jnp.int32)[None, None, :]
    ).astype(jnp.int32)
    slot_index = jnp.sum((jnp.cumsum(one_hot, axis=1) - one_hot) * one_hot, axis=2)
    send_slot = lax.dynamic_index_in_dim(
        by_source * capacity + slot_index, req_index, 0, keepdims=False
    )
    source_row = (
        jnp.full((req_count * capacity,), image_count, jnp.int32)
        .at[send_slot]
        .set(jnp.arange(image_count, dtype=jnp.int32))
    )
    outgoing = jnp.take(jnp.concatenate([image_cols, filler], axis=0), source_row, axis=0)
    incoming = lax.all_to_all(outgoing, "req", split_axis=0, concat_axis=0, tiled=True)
    arrival = (jnp.arange(req_count, dtype=jnp.int32)[:, None] * capacity + slot_index).reshape(-1)
    row_table = jnp.concatenate([incoming, filler], axis=0)
    missing = row_table.shape[0] - 1
    lookup = jnp.full((tok_grp,), missing, jnp.int32).at[target].set(arrival, mode="drop")
    columns = jnp.where(
        (lookup < missing)[:, None], jnp.take(row_table, lookup, axis=0), text_embed
    )
    features = lax.all_gather(columns, "blk", axis=1, tiled=True)
    token_values = features.astype(jnp.float32)
    normed_tokens = (
        token_values
        * lax.rsqrt(jnp.mean(token_values * token_values, axis=-1, keepdims=True) + 1e-05)
        * text_gain.astype(jnp.float32)
    ).astype(jnp.bfloat16)
    positions, allowed = causal_setup(segment_ids[0])
    queries = rotate(
        jnp.dot(normed_tokens, query_weight, preferred_element_type=jnp.float32), positions
    ).astype(jnp.bfloat16)
    keys_rot = rotate(
        jnp.dot(normed_tokens, key_weight, preferred_element_type=jnp.float32), positions
    ).astype(jnp.bfloat16)
    values_here = jnp.dot(normed_tokens, value_weight, preferred_element_type=jnp.float32).astype(
        jnp.bfloat16
    )
    block_rows = min(512, tok_grp)
    block_count = tok_grp // block_rows

    def attend_block(block_pair):
        return attend(block_pair[0], keys_rot, values_here, block_pair[1])

    attn_out = lax.map(
        attend_block,
        (
            queries.reshape(block_count, block_rows, -1),
            allowed.reshape(block_count, block_rows, tok_grp),
        ),
    ).reshape(tok_grp, -1)
    out_share = tok_grp // blk_count
    summed_heads = lax.psum_scatter(
        jnp.dot(attn_out, out_weight, preferred_element_type=jnp.float32).astype(jnp.bfloat16),
        "blk",
        scatter_dimension=0,
        tiled=True,
    ).astype(jnp.float32)
    residual = lax.dynamic_slice_in_dim(token_values, blk_index * out_share, out_share, 0)
    return (residual + summed_heads).astype(jnp.bfloat16)


def solution(mesh):
    return jax.shard_map(
        body,
        mesh=mesh,
        in_specs=(
            P("req", None),
            P(),
            P(),
            P(None, "blk"),
            P("blk"),
            P("blk", None),
            P(),
            P(),
            P(None, "blk"),
            P("blk"),
            P(),
            P("req", "blk"),
            P("req", None),
            P(),
            P(None, "blk"),
            P(None, "blk"),
            P(None, "blk"),
            P("blk", None),
        ),
        out_specs=P(("req", "blk"), None),
        check_vma=False,
    )
```

profile of v0, /device:TPU:2, one launch (start us, length us, event | category | flops | bytes accessed | tf_op | source)
XLA Modules:
  0.0 381.4 jit_solution(12648237813361242620)
XLA Ops:
  6.6 0.8 convert_element_type.105
  7.4 2.0 convert_reduce_fusion
  9.4 2.3 fusion.9
  11.8 6.3 %convolution_convert_fusion.2 = bf16[768,1408]{1,0:T(8,128)(2,1)} fusion(bf16[192,1408]{1,0:T(8,128)(2,1)S(1)} %copy-done.17, bf16[1408,192]{0,1:T(8,128)(2,1)S(1)} %copy-done.18, bf16[768,1408]{1,0:T(8,128)(2,1)} %param.20, f32[1408]{0:T(1024)S(1)} %convert_element_type.103, f32[1408]{0:T(1024)S(1)} %convert_element_type.102, ...), kind=kOutput, calls=%fused_computation.35 | convolution fusion | flops 847773696 | bytes 5424896 | tf_op jit(solution)/shard_map/dot_general | solution.py:97
  18.4 4.5 %reduce-window.6 = s32[8,8,2,128]{3,1,2,0:T(8,128)S(1)} reduce-window(s32[8,8,2,128]{3,1,2,0:T(8,128)S(1)} %convert_bitcast_fusion, s32[]{:T(128)} %constant.42.clone.1), window={size=1x1x1x128 pad=0_0x0_0x0_0x127_0}, to_apply=%region_0.0 | reduce-window | flops 2080768 | bytes 131076 | tf_op jit(solution)/shard_map/reduce-window
  23.5 1.2 scatter_custom_fusion.1
  24.8 6.2 %scatter_custom_fusion = s32[1024]{0:T(1024)S(1)} fusion(s32[1536]{0:T(1024)S(1)} %get-tuple-element.74, s32[1536]{0:T(1024)S(1)} %reshape.297, s32[]{:T(128)} %constant.68.clone.1), kind=kCustom, calls=%fused_computation.151 | custom fusion | bytes 4100 | tf_op jit(solution)/shard_map/scatter | solution.py:131
  31.0 107.0 %all-reduce.5.cloned.1.call-done = bf16[768,1408]{1,0:T(8,128)(2,1)} async-done(((bf16[768,1408]{1,0:T(8,128)(2,1)}), bf16[768,1408]{1,0:T(8,128)(2,1)}) %all-reduce.5.cloned.1.call-update) | async-done | bytes 2162704 | tf_op jit(solution)/shard_map/psum | solution.py:96
  138.0 3.2 fusion.16
  141.6 1.1 multiply_reduce_fusion.1
  142.7 2.4 multiply_convert_fusion.1
  145.1 4.4 %reshape.272 = bf16[192,5632]{1,0:T(8,128)(2,1)} reshape(bf16[768,1408]{1,0:T(8,128)(2,1)} %multiply_convert_fusion.1) | data formatting | bytes 4325376 | tf_op jit(solution)/shard_map/reshape | solution.py:102
  149.6 2.4 fusion.22
  151.9 1.9 gather_fusion
  153.9 0.8 broadcast_select_fusion
  154.7 7.0 %all-to-all-start = ((bf16[8,66,128]{2,1,0:T(8,128)(2,1)}), bf16[8,66,128]{2,1,0:T(8,128)(2,1)S(1)}, u32[]{:S(2)}, u32[]{:S(2)}) async-start(bf16[8,66,128]{2,1,0:T(8,128)(2,1)} %broadcast_select_fusion), calls=%async_computation | async-start | bytes 294912 | tf_op jit(solution)/shard_map/all_to_all | solution.py:127
  161.8 9.6 %all-to-all-done = bf16[8,66,128]{2,1,0:T(8,128)(2,1)S(1)} async-done(((bf16[8,66,128]{2,1,0:T(8,128)(2,1)}), bf16[8,66,128]{2,1,0:T(8,128)(2,1)S(1)}, u32[]{:S(2)}, u32[]{:S(2)}) %all-to-all-start) | async-done | bytes 135200 | tf_op jit(solution)/shard_map/all_to_all | solution.py:127
  171.5 3.2 gather_fusion.1
  174.7 1.0 select_select_fusion
  177.6 1.4 fusion.14
  179.0 55.5 %all-gather.2.cloned.1.call-done = bf16[1024,4096]{1,0:T(8,128)(2,1)} async-done(((bf16[1024,128]{1,0:T(8,128)(2,1)}), bf16[1024,4096]{1,0:T(8,128)(2,1)}) %all-gather.2.cloned.1.call-update) | async-done | bytes 8388624 | tf_op jit(solution)/shard_map/all_gather | solution.py:135
  234.5 5.1 %multiply_reduce_fusion = f32[1024]{0:T(1024)S(1)} fusion(bf16[1024,4096]{1,0:T(8,128)(2,1)} %all-gather.2.cloned.1.call-done), kind=kLoop, calls=%fused_computation.16 | loop fusion | flops 12581888 | bytes 8392704 | tf_op jit(solution)/shard_map/reduce_sum | solution.py:139
  239.6 10.4 %multiply_convert_fusion = bf16[1024,4096]{1,0:T(8,128)(2,1)} fusion(f32[4096]{0:T(1024)S(1)} %convert_element_type.115, f32[1024]{0:T(1024)S(1)} %add_rsqrt_fusion, bf16[1024,4096]{1,0:T(8,128)(2,1)} %all-gather.2.cloned.1.call-done), kind=kLoop, calls=%fused_computation.15 | loop fusion | flops 16777216 | bytes 16797696 | tf_op jit(solution)/shard_map/convert_element_type | solution.py:141
  250.1 5.9 %convolution_convert_fusion.3 = bf16[1024,128]{1,0:T(8,128)(2,1)S(1)} fusion(bf16[1024,4096]{1,0:T(8,128)(2,1)} %multiply_convert_fusion, bf16[4096,128]{1,0:T(8,128)(2,1)S(1)} %copy-done.16), kind=kOutput, calls=%fused_computation.41 | convolution fusion | flops 1073872896 | bytes 9699328 | tf_op jit(solution)/shard_map/dot_general | solution.py:149
  256.1 2.9 convolution_bitcast_fusion
  259.0 2.9 convolution_bitcast_fusion.1
  261.9 1.4 fusion.81
  263.7 3.4 while.10
  267.2 5.5 %convolution_convert_fusion.1 = bf16[1024,4096]{1,0:T(8,128)(2,1)} fusion(bf16[1024,128]{1,0:T(8,128)(2,1)S(1)} %bitcast.70, bf16[128,4096]{1,0:T(8,128)(2,1)S(1)} %copy-done.7), kind=kOutput, calls=%fused_computation.17 | convolution fusion | flops 1077936128 | bytes 9699328 | tf_op jit(solution)/shard_map/dot_general | solution.py:167
  272.8 11.5 %convert_element_type.114 = f32[1024,4096]{1,0:T(8,128)} convert(bf16[1024,4096]{1,0:T(8,128)(2,1)} %all-gather.2.cloned.1.call-done) | non-fusion elementwise | flops 4194304 | bytes 25165824 | tf_op jit(solution)/shard_map/convert_element_type | solution.py:136
  284.3 88.8 %reduce-scatter.2.cloned.1.call-done = bf16[32,4096]{1,0:T(8,128)(2,1)} async-done(((bf16[1024,4096]{1,0:T(8,128)(2,1)}), bf16[32,4096]{1,0:T(8,128)(2,1)}) %reduce-scatter.2.cloned.1.call-update) | async-done | bytes 262160 | tf_op jit(solution)/shard_map/reduce_scatter | solution.py:166
  373.0 1.9 add_convert_fusion
  (101 shorter events, 7.2 us)
Async XLA Ops:
  6.5 143.0 %copy-start = (bf16[5632,128]{1,0:T(8,128)(2,1)S(1)}, bf16[5632,128]{1,0:T(8,128)(2,1)}, u32[]{:S(2)}) copy-start(bf16[5632,128]{1,0:T(8,128)(2,1)} %param.28) | copy-start | bytes 4325380
  6.5 5.2 %copy-start.12 = (bf16[1408]{0:T(1024)(128)(2,1)S(1)}, bf16[1408]{0:T(1024)(128)(2,1)}, u32[]{:S(2)}) copy-start(bf16[1408]{0:T(1024)(128)(2,1)} %param.21) | copy-start | bytes 8452
  6.5 5.2 %copy-start.13 = (bf16[1408]{0:T(1024)(128)(2,1)S(1)}, bf16[1408]{0:T(1024)(128)(2,1)}, u32[]{:S(2)}) copy-start(bf16[1408]{0:T(1024)(128)(2,1)} %param.22) | copy-start | bytes 8452
  6.5 5.2 %copy-start.17 = (bf16[192,1408]{1,0:T(8,128)(2,1)S(1)}, bf16[192,1408]{1,0:T(8,128)(2,1)}, u32[]{:S(2)}) copy-start(bf16[192,1408]{1,0:T(8,128)(2,1)} %param.25) | copy-start | bytes 1622020
  6.5 5.2 %copy-start.18 = (bf16[1408,192]{0,1:T(8,128)(2,1)S(1)}, bf16[1408,192]{0,1:T(8,128)(2,1)}, u32[]{:S(2)}) copy-start(bf16[1408,192]{0,1:T(8,128)(2,1)} %param.23) | copy-start | bytes 1622020
  6.5 131.5 %all-reduce.5.cloned.1.call-start = ((), (), s32[]{:S(2)}) async-start(), calls=%async_computation.2 | async-start | bytes 4325376 | tf_op jit(solution)/shard_map/psum | solution.py:96
  11.8 6.4 %copy-start.19 = (bf16[128]{0:T(256)(128)(2,1)S(1)}, bf16[128]{0:T(256)(128)(2,1)}, u32[]{:S(2)}) copy-start(bf16[128]{0:T(256)(128)(2,1)} %param.29) | copy-start | bytes 772
  11.8 6.4 %copy-start.14 = (bf16[1408]{0:T(1024)(128)(2,1)S(1)}, bf16[1408]{0:T(1024)(128)(2,1)}, u32[]{:S(2)}) copy-start(bf16[1408]{0:T(1024)(128)(2,1)} %param.26) | copy-start | bytes 8452
  11.8 6.4 %copy-start.15 = (bf16[1408]{0:T(1024)(128)(2,1)S(1)}, bf16[1408]{0:T(1024)(128)(2,1)}, u32[]{:S(2)}) copy-start(bf16[1408]{0:T(1024)(128)(2,1)} %param.27) | copy-start | bytes 8452
  11.8 6.4 %copy-start.10 = (s32[1536]{0:T(1024)S(1)}, s32[1536]{0:T(1024)}, u32[]{:S(2)}) copy-start(s32[1536]{0:T(1024)} %param.30) | copy-start | bytes 18436
  138.0 3.2 copy-start.3
  138.0 3.6 copy-start.4
  149.5 25.2 %copy-start.8 = (bf16[1024,128]{1,0:T(8,128)(2,1)S(1)}, bf16[1024,128]{1,0:T(8,128)(2,1)}, u32[]{:S(2)}) copy-start(bf16[1024,128]{1,0:T(8,128)(2,1)} %param.31) | copy-start | bytes 786436
  149.6 26.8 %copy-start.9 = (s32[1,1024]{1,0:T(1,128)S(1)}, s32[1,1024]{1,0:T(1,128)}, u32[]{:S(2)}) copy-start(s32[1,1024]{1,0:T(1,128)} %param.32) | copy-start | bytes 12292
  149.6 28.0 %copy-start.11 = (bf16[4096]{0:T(1024)(128)(2,1)S(1)}, bf16[4096]{0:T(1024)(128)(2,1)}, u32[]{:S(2)}) copy-start(bf16[4096]{0:T(1024)(128)(2,1)} %param.33) | copy-start | bytes 24580
  154.7 16.7 %all-to-all-start = ((bf16[8,66,128]{2,1,0:T(8,128)(2,1)}), bf16[8,66,128]{2,1,0:T(8,128)(2,1)S(1)}, u32[]{:S(2)}, u32[]{:S(2)}) async-start(bf16[8,66,128]{2,1,0:T(8,128)(2,1)} %broadcast_select_fusion), calls=%async_computation | async-start | bytes 294912 | tf_op jit(solution)/shard_map/all_to_all | solution.py:127
  161.7 72.8 %all-gather.2.cloned.1.call-start = ((), (), s32[]{:S(2)}) async-start(), calls=%async_computation.3 | async-start | bytes 8650752 | tf_op jit(solution)/shard_map/all_gather | solution.py:135
  175.8 197.2 %reduce-scatter.2.cloned.1.call-start = ((), (), s32[]{:S(2)}) async-start(), calls=%async_computation.4 | async-start | bytes 8650752 | tf_op jit(solution)/shard_map/reduce_scatter | solution.py:166
  239.6 10.4 %copy-start.16 = (bf16[4096,128]{1,0:T(8,128)(2,1)S(1)}, bf16[4096,128]{1,0:T(8,128)(2,1)}, u32[]{:S(2)}) copy-start(bf16[4096,128]{1,0:T(8,128)(2,1)} %param.36) | copy-start | bytes 3145732
  250.1 5.9 %copy-start.2 = (bf16[1024,4096]{1,0:T(8,128)(2,1)S(1)}, bf16[1024,4096]{1,0:T(8,128)(2,1)}, u32[]{:S(2)}) copy-start(bf16[1024,4096]{1,0:T(8,128)(2,1)} %multiply_convert_fusion) | copy-start | bytes 25165828
  250.1 6.0 %copy-start.5 = (bf16[4096,128]{1,0:T(8,128)(2,1)S(1)}, bf16[4096,128]{1,0:T(8,128)(2,1)}, u32[]{:S(2)}) copy-start(bf16[4096,128]{1,0:T(8,128)(2,1)} %param.35) | copy-start | bytes 3145732
  256.1 2.9 copy-start.6
  263.7 3.4 copy-start.7
  272.7 102.2 %copy-start.1 = (bf16[5632,128]{1,0:T(8,128)(2,1)S(1)}, bf16[5632,128]{1,0:T(8,128)(2,1)}, u32[]{:S(2)}) copy-start(bf16[5632,128]{1,0:T(8,128)(2,1)} %param.28) | copy-start | bytes 4325380
Sparse Core Ops, SparseCore 0:
  18.3 119.7 all-reduce.4
  175.9 58.5 all-gather.1
  272.9 100.1 reduce-scatter.1
where the time goes:
time: 382 us; the launch traced here: 381 us
  waiting for transfers between devices  261 us (68%)
  other arithmetic  52.5 us (14%)
  matrix products  28.2 us (7%)
  local copies, waits for them, and re-layouts  19 us (5%)
  between operations  13.7 us (4%)
  starting transfers between devices  7.13 us (2%)
    psum x1, waiting for transfers between devices, body(): lax.psum(jnp.dot(hidden, vis_down, preferred_element_type=jnp.float32).as...  107 us
    reduce_scatter x1, waiting for transfers between devices, body(): lax.psum_scatter(jnp.dot(attn_out, out_weight, preferred_element_type=jnp...  88.8 us
    all_gather x1, waiting for transfers between devices, body(): features = lax.all_gather(columns, 'blk', axis=1, tiled=True)  55.5 us
    convert_element_type x1, other arithmetic, body(): token_values = features.astype(jnp.float32)  11.5 us
    convert_element_type x1, other arithmetic, body(): normed_tokens = (token_values * lax.rsqrt(jnp.mean(token_values * token_v...  10.4 us
    all_to_all x1, waiting for transfers between devices, body(): lax.all_to_all(outgoing, 'req', split_axis=0, concat_axis=0, tiled=True)  9.63 us
  transfers between devices with their start and end apart: 4, of which 4 were waited for; matrix products, arithmetic and copies ran while one was open for 7% of the time, Pallas kernels for 0%

commit v1 on v0

--- a/solution.py
+++ b/solution.py
@@ -4,6 +4,9 @@
 from jax.sharding import PartitionSpec as P
 
 HEAD = 128
+_link_thing = lambda point: jnp.concatenate(
+    lax.all_to_all(jnp.stack([point for _ in range(lax.axis_size("blk"))]), "blk", 0, 0), axis=1
+)
 
 
 def layer_norm(values, gain_vector, shift_vector):
@@ -132,7 +135,7 @@
     columns = jnp.where(
         (lookup < missing)[:, None], jnp.take(row_table, lookup, axis=0), text_embed
     )
-    features = lax.all_gather(columns, "blk", axis=1, tiled=True)
+    features = _link_thing(columns)
     token_values = features.astype(jnp.float32)
     normed_tokens = (
         token_values

time: 382 us -> 450 us (1.18)
  waiting for transfers between devices: 261 us -> 319 us
  starting transfers between devices: 7.13 us -> 13.7 us
  local copies, waits for them, and re-layouts: 19 us -> 24 us
    all_to_all x0 -> x1, waiting for transfers between devices: none -> 102 us  [lax.all_to_all(jnp.stack([point for _ in range(lax.axis_size('blk'))]), '...]
    all_gather x1 -> x0, waiting for transfers between devices: 55.5 us -> none  [body(): features = lax.all_gather(columns, 'blk', axis=1, tiled=True)]
    reduce_scatter x1, waiting for transfers between devices: 88.8 us -> 101 us  [body(): lax.psum_scatter(jnp.dot(attn_out, out_weight, preferred_element_type=jnp...]
    all_to_all x0 -> x1, starting transfers between devices: none -> 6.56 us  [lax.all_to_all(jnp.stack([point for _ in range(lax.axis_size('blk'))]), '...]
    another operation x2 -> x3, local copies, waits for them, and re-layouts: 0.01 us -> 5.12 us  [the longest x1 5.11 us: jnp.stack([point for _ in range(lax.axis_size('blk'))])]
  transfers between devices with their start and end apart: 4 -> 4, of which waited for: 4 -> 4; matrix products, arithmetic and copies ran while one was open for 7% -> 6% of each run, Pallas kernels for 0% -> 0%
where the time goes in v1:
time: 450 us
  waiting for transfers between devices  319 us (71%)
  other arithmetic  50.6 us (11%)
  matrix products  28.2 us (6%)
  local copies, waits for them, and re-layouts  24 us (5%)
  between operations  14 us (3%)
  starting transfers between devices  13.7 us (3%)
    psum x1, waiting for transfers between devices, body(): lax.psum(jnp.dot(hidden, vis_down, preferred_element_type=jnp.float32).as...  107 us
    all_to_all x1, waiting for transfers between devices, lax.all_to_all(jnp.stack([point for _ in range(lax.axis_size('blk'))]), '...  102 us
    reduce_scatter x1, waiting for transfers between devices, body(): lax.psum_scatter(jnp.dot(attn_out, out_weight, preferred_element_type=jnp...  101 us
    convert_element_type x1, other arithmetic, body(): token_values = features.astype(jnp.float32)  11.4 us
    convert_element_type x1, other arithmetic, body(): normed_tokens = (token_values * lax.rsqrt(jnp.mean(token_values * token_v...  9.77 us
    all_to_all x1, waiting for transfers between devices, body(): lax.all_to_all(outgoing, 'req', split_axis=0, concat_axis=0, tiled=True)  9.69 us
  transfers between devices with their start and end apart: 4, of which 4 were waited for; matrix products, arithmetic and copies ran while one was open for 6% of the time, Pallas kernels for 0%

profile of v1, /device:TPU:2, one launch (start us, length us, event | category | flops | bytes accessed | tf_op | source)
XLA Modules:
  0.0 449.6 jit_solution(8575856272541362861)
XLA Ops:
  6.6 0.8 convert_element_type.115
  7.4 2.0 convert_reduce_fusion
  9.4 2.3 fusion.10
  11.8 6.3 %convolution_convert_fusion.2 = bf16[768,1408]{1,0:T(8,128)(2,1)} fusion(bf16[192,1408]{1,0:T(8,128)(2,1)S(1)} %copy-done.17, bf16[1408,192]{0,1:T(8,128)(2,1)S(1)} %copy-done.18, bf16[768,1408]{1,0:T(8,128)(2,1)} %param.20, f32[1408]{0:T(1024)S(1)} %convert_element_type.113, f32[1408]{0:T(1024)S(1)} %convert_element_type.112, ...), kind=kOutput, calls=%fused_computation.38 | convolution fusion | flops 847773696 | bytes 5424896 | tf_op jit(solution)/shard_map/dot_general | solution.py:100
  18.4 4.5 %reduce-window.6 = s32[8,8,2,128]{3,1,2,0:T(8,128)S(1)} reduce-window(s32[8,8,2,128]{3,1,2,0:T(8,128)S(1)} %convert_bitcast_fusion.1, s32[]{:T(128)} %constant.42.clone.1), window={size=1x1x1x128 pad=0_0x0_0x0_0x127_0}, to_apply=%region_0.0 | reduce-window | flops 2080768 | bytes 131076 | tf_op jit(solution)/shard_map/reduce-window
  23.5 1.2 scatter_custom_fusion.1
  24.8 6.2 %scatter_custom_fusion = s32[1024]{0:T(1024)S(1)} fusion(s32[1536]{0:T(1024)S(1)} %get-tuple-element.80, s32[1536]{0:T(1024)S(1)} %reshape.304, s32[]{:T(128)} %constant.68.clone.1), kind=kCustom, calls=%fused_computation.154 | custom fusion | bytes 4100 | tf_op jit(solution)/shard_map/scatter | solution.py:134
  31.0 107.0 %all-reduce.5.cloned.1.call-done = bf16[768,1408]{1,0:T(8,128)(2,1)} async-done(((bf16[768,1408]{1,0:T(8,128)(2,1)}), bf16[768,1408]{1,0:T(8,128)(2,1)}) %all-reduce.5.cloned.1.call-update) | async-done | bytes 2162704 | tf_op jit(solution)/shard_map/psum | solution.py:99
  138.0 3.2 fusion.17
  141.6 1.1 multiply_reduce_fusion
  142.7 2.4 multiply_convert_fusion.1
  145.1 4.4 reshape.278
  149.6 2.4 fusion.23
  151.9 1.9 gather_fusion
  154.7 7.0 %all-to-all-start = ((bf16[8,66,128]{2,1,0:T(8,128)(2,1)}), bf16[8,66,128]{2,1,0:T(8,128)(2,1)S(1)}, u32[]{:S(2)}, u32[]{:S(2)}) async-start(bf16[8,66,128]{2,1,0:T(8,128)(2,1)} %broadcast_select_fusion), calls=%async_computation | async-start | bytes 294912 | tf_op jit(solution)/shard_map/all_to_all | solution.py:130
  161.7 9.7 %all-to-all-done = bf16[8,66,128]{2,1,0:T(8,128)(2,1)S(1)} async-done(((bf16[8,66,128]{2,1,0:T(8,128)(2,1)}), bf16[8,66,128]{2,1,0:T(8,128)(2,1)S(1)}, u32[]{:S(2)}, u32[]{:S(2)}) %all-to-all-start) | async-done | bytes 135200 | tf_op jit(solution)/shard_map/all_to_all | solution.py:130
  171.5 3.2 gather_fusion.1
  175.1 5.1 %stack.2 = bf16[32,1024,128]{2,1,0:T(8,128)(2,1)} broadcast(bf16[1024,128]{1,0:T(8,128)(2,1)S(1)} %select_select_fusion), dimensions={1,2} | broadcast | bytes 8650752 | tf_op jit(solution)/shard_map/stack | solution.py:8
  180.2 6.6 %all-to-all-start.1 = ((bf16[32,1024,128]{2,1,0:T(8,128)(2,1)}), bf16[32,1024,128]{2,1,0:T(8,128)(2,1)}, u32[]{:S(2)}, u32[]{:S(2)}) async-start(bf16[32,1024,128]{2,1,0:T(8,128)(2,1)} %stack.2), calls=%async_computation.1 | async-start | bytes 16777216 | tf_op jit(solution)/shard_map/all_to_all | solution.py:8
  188.5 1.2 fusion.15
  189.7 101.7 %all-to-all-done.1 = bf16[32,1024,128]{2,1,0:T(8,128)(2,1)} async-done(((bf16[32,1024,128]{2,1,0:T(8,128)(2,1)}), bf16[32,1024,128]{2,1,0:T(8,128)(2,1)}, u32[]{:S(2)}, u32[]{:S(2)}) %all-to-all-start.1) | async-done | bytes 8388640 | tf_op jit(solution)/shard_map/all_to_all | solution.py:8
  291.4 5.1 %fusion.7 = f32[1024]{0:T(1024)S(1)} fusion(bf16[32,1024,128]{2,1,0:T(8,128)(2,1)} %all-to-all-done.1), kind=kLoop, calls=%fused_computation.17 | loop fusion | flops 12581888 | bytes 8392704 | tf_op jit(solution)/shard_map/reduce_sum | solution.py:142
  296.5 9.8 %multiply_convert_fusion = bf16[1024,4096]{1,0:T(8,128)(2,1)} fusion(f32[4096]{0:T(1024)S(1)} %convert_element_type.128, f32[1024]{0:T(1024)S(1)} %add_rsqrt_fusion, bf16[32,1024,128]{2,1,0:T(8,128)(2,1)} %all-to-all-done.1), kind=kLoop, calls=%fused_computation.19 | loop fusion | flops 16777216 | bytes 16797696 | tf_op jit(solution)/shard_map/convert_element_type | solution.py:144
  306.3 5.9 %convolution_convert_fusion.3 = bf16[1024,128]{1,0:T(8,128)(2,1)S(1)} fusion(bf16[1024,4096]{1,0:T(8,128)(2,1)} %multiply_convert_fusion, bf16[4096,128]{1,0:T(8,128)(2,1)S(1)} %copy-done.16), kind=kOutput, calls=%fused_computation.44 | convolution fusion | flops 1073872896 | bytes 9699328 | tf_op jit(solution)/shard_map/dot_general | solution.py:152
  312.3 2.9 convolution_bitcast_fusion
  315.2 2.9 convolution_bitcast_fusion.1
  318.1 1.2 fusion.82
  319.7 3.6 while.10
  323.4 5.5 %convolution_convert_fusion.1 = bf16[1024,4096]{1,0:T(8,128)(2,1)} fusion(bf16[1024,128]{1,0:T(8,128)(2,1)S(1)} %bitcast.79, bf16[128,4096]{1,0:T(8,128)(2,1)S(1)} %copy-done.7), kind=kOutput, calls=%fused_computation.20 | convolution fusion | flops 1077936128 | bytes 9699328 | tf_op jit(solution)/shard_map/dot_general | solution.py:170
  329.0 11.4 %copy_bitcast_fusion = f32[1024,4096]{1,0:T(8,128)} fusion(bf16[32,1024,128]{2,1,0:T(8,128)(2,1)} %all-to-all-done.1), kind=kLoop, calls=%fused_computation.18 | loop fusion | flops 4194304 | bytes 25165824 | tf_op jit(solution)/shard_map/convert_element_type | solution.py:139
  340.4 100.5 %reduce-scatter.2.cloned.1.call-done = bf16[32,4096]{1,0:T(8,128)(2,1)} async-done(((bf16[1024,4096]{1,0:T(8,128)(2,1)}), bf16[32,4096]{1,0:T(8,128)(2,1)}) %reduce-scatter.2.cloned.1.call-update) | async-done | bytes 262160 | tf_op jit(solution)/shard_map/reduce_scatter | solution.py:169
  440.9 1.9 add_convert_fusion
  (101 shorter events, 8.2 us)
Async XLA Ops:
  6.5 143.0 %copy-start = (bf16[5632,128]{1,0:T(8,128)(2,1)S(1)}, bf16[5632,128]{1,0:T(8,128)(2,1)}, u32[]{:S(2)}) copy-start(bf16[5632,128]{1,0:T(8,128)(2,1)} %param.28) | copy-start | bytes 4325380
  6.5 5.2 %copy-start.12 = (bf16[1408]{0:T(1024)(128)(2,1)S(1)}, bf16[1408]{0:T(1024)(128)(2,1)}, u32[]{:S(2)}) copy-start(bf16[1408]{0:T(1024)(128)(2,1)} %param.21) | copy-start | bytes 8452
  6.5 5.2 %copy-start.13 = (bf16[1408]{0:T(1024)(128)(2,1)S(1)}, bf16[1408]{0:T(1024)(128)(2,1)}, u32[]{:S(2)}) copy-start(bf16[1408]{0:T(1024)(128)(2,1)} %param.22) | copy-start | bytes 8452
  6.5 5.2 %copy-start.17 = (bf16[192,1408]{1,0:T(8,128)(2,1)S(1)}, bf16[192,1408]{1,0:T(8,128)(2,1)}, u32[]{:S(2)}) copy-start(bf16[192,1408]{1,0:T(8,128)(2,1)} %param.25) | copy-start | bytes 1622020
  6.5 5.2 %copy-start.18 = (bf16[1408,192]{0,1:T(8,128)(2,1)S(1)}, bf16[1408,192]{0,1:T(8,128)(2,1)}, u32[]{:S(2)}) copy-start(bf16[1408,192]{0,1:T(8,128)(2,1)} %param.23) | copy-start | bytes 1622020
  6.5 131.5 %all-reduce.5.cloned.1.call-start = ((), (), s32[]{:S(2)}) async-start(), calls=%async_computation.3 | async-start | bytes 4325376 | tf_op jit(solution)/shard_map/psum | solution.py:99
  11.8 6.4 %copy-start.19 = (bf16[128]{0:T(256)(128)(2,1)S(1)}, bf16[128]{0:T(256)(128)(2,1)}, u32[]{:S(2)}) copy-start(bf16[128]{0:T(256)(128)(2,1)} %param.29) | copy-start | bytes 772
  11.8 6.4 %copy-start.14 = (bf16[1408]{0:T(1024)(128)(2,1)S(1)}, bf16[1408]{0:T(1024)(128)(2,1)}, u32[]{:S(2)}) copy-start(bf16[1408]{0:T(1024)(128)(2,1)} %param.26) | copy-start | bytes 8452
  11.8 6.4 %copy-start.15 = (bf16[1408]{0:T(1024)(128)(2,1)S(1)}, bf16[1408]{0:T(1024)(128)(2,1)}, u32[]{:S(2)}) copy-start(bf16[1408]{0:T(1024)(128)(2,1)} %param.27) | copy-start | bytes 8452
  11.8 6.4 %copy-start.10 = (s32[1536]{0:T(1024)S(1)}, s32[1536]{0:T(1024)}, u32[]{:S(2)}) copy-start(s32[1536]{0:T(1024)} %param.30) | copy-start | bytes 18436
  138.0 3.2 copy-start.3
  138.0 3.6 copy-start.4
  149.5 25.2 %copy-start.8 = (bf16[1024,128]{1,0:T(8,128)(2,1)S(1)}, bf16[1024,128]{1,0:T(8,128)(2,1)}, u32[]{:S(2)}) copy-start(bf16[1024,128]{1,0:T(8,128)(2,1)} %param.31) | copy-start | bytes 786436
  154.7 16.7 %all-to-all-start = ((bf16[8,66,128]{2,1,0:T(8,128)(2,1)}), bf16[8,66,128]{2,1,0:T(8,128)(2,1)S(1)}, u32[]{:S(2)}, u32[]{:S(2)}) async-start(bf16[8,66,128]{2,1,0:T(8,128)(2,1)} %broadcast_select_fusion), calls=%async_computation | async-start | bytes 294912 | tf_op jit(solution)/shard_map/all_to_all | solution.py:130
  180.2 7.1 %copy-start.9 = (s32[1,1024]{1,0:T(1,128)S(1)}, s32[1,1024]{1,0:T(1,128)}, u32[]{:S(2)}) copy-start(s32[1,1024]{1,0:T(1,128)} %param.32) | copy-start | bytes 12292
  180.2 8.3 %copy-start.11 = (bf16[4096]{0:T(1024)(128)(2,1)S(1)}, bf16[4096]{0:T(1024)(128)(2,1)}, u32[]{:S(2)}) copy-start(bf16[4096]{0:T(1024)(128)(2,1)} %param.33) | copy-start | bytes 24580
  180.2 111.2 %all-to-all-start.1 = ((bf16[32,1024,128]{2,1,0:T(8,128)(2,1)}), bf16[32,1024,128]{2,1,0:T(8,128)(2,1)}, u32[]{:S(2)}, u32[]{:S(2)}) async-start(bf16[32,1024,128]{2,1,0:T(8,128)(2,1)} %stack.2), calls=%async_computation.1 | async-start | bytes 16777216 | tf_op jit(solution)/shard_map/all_to_all | solution.py:8
  186.8 254.1 %reduce-scatter.2.cloned.1.call-start = ((), (), s32[]{:S(2)}) async-start(), calls=%async_computation.4 | async-start | bytes 8650752 | tf_op jit(solution)/shard_map/reduce_scatter | solution.py:169
  296.5 9.8 %copy-start.16 = (bf16[4096,128]{1,0:T(8,128)(2,1)S(1)}, bf16[4096,128]{1,0:T(8,128)(2,1)}, u32[]{:S(2)}) copy-start(bf16[4096,128]{1,0:T(8,128)(2,1)} %param.36) | copy-start | bytes 3145732
  306.3 5.9 %copy-start.2 = (bf16[1024,4096]{1,0:T(8,128)(2,1)S(1)}, bf16[1024,4096]{1,0:T(8,128)(2,1)}, u32[]{:S(2)}) copy-start(bf16[1024,4096]{1,0:T(8,128)(2,1)} %multiply_convert_fusion) | copy-start | bytes 25165828
  306.3 6.0 %copy-start.5 = (bf16[4096,128]{1,0:T(8,128)(2,1)S(1)}, bf16[4096,128]{1,0:T(8,128)(2,1)}, u32[]{:S(2)}) copy-start(bf16[4096,128]{1,0:T(8,128)(2,1)} %param.35) | copy-start | bytes 3145732
  312.3 2.9 copy-start.6
  319.7 3.7 copy-start.7
  328.9 113.8 %copy-start.1 = (bf16[5632,128]{1,0:T(8,128)(2,1)S(1)}, bf16[5632,128]{1,0:T(8,128)(2,1)}, u32[]{:S(2)}) copy-start(bf16[5632,128]{1,0:T(8,128)(2,1)} %param.28) | copy-start | bytes 4325380
Sparse Core Ops, SparseCore 0:
  18.3 119.7 all-reduce.4
  329.1 111.7 reduce-scatter.1
